TPU v7x, 32 devices: a whole 2x2x4 slice. The times are simulated.
32 devices in a mesh: grp: 8 (over y, x, core), sub: 4 (over z).
Axes of the slice: x: 2, y: 2, z: 4, core: 2. Of those that a mesh axis runs over, the one named last changes fastest.
Arguments:
- tokens: bfloat16 [128, 32, 256], P(('grp', 'sub')), may hold values from -64 to 64
- proj_weight: bfloat16 [256, 256], replicated, may hold values from -2 to 2
- match_grad: bfloat16 [4096, 1024], P(('grp', 'sub')), may hold values from -3072 to 3072
- edge_first: int32 [4096], P(('grp', 'sub')), may hold values from 0 to 15, as said below
- pair_second_image: int32 [4096], P(('grp', 'sub')), may hold values from 0 to 31, as said below
- send_pick: int32 [1024], P(('grp', 'sub')), may hold values from 0 to 3, as said below
Outputs:
- token_grad: bfloat16 [128, 32, 256], P(('grp', 'sub'))
Inputs may be any that keep to these rules, and one draw needn't show every extreme that they name: On each device the pairs (edge_first, pair_second_image) are distinct. `pair_second_image`: on each device every receive slot 0 to 31 is named by at least one pair. `send_pick`: for each device and each index p of grp, the 4 entries of its send slots p * 4 to p * 4 + 3 name different images.
All inputs are finite; a program needn't handle non-finite values.
Results may differ from a plain program's by a relative error of at most 0.017.
Values may be sent and summed in bfloat16 or wider, within the bound.
No kernel may reach another device: no remote copies, remote signals or barrier semaphores. Data moves between devices by JAX's collectives and lax.ppermute only.
A program may use at most 64 MiB of HBM per device.

v0:
```python
import jax
import jax.numpy as jnp
from jax import lax
from jax.sharding import PartitionSpec as P

EPSILON = 1e-05
SOFTMAX_COOLING = 0.1


def normalize(token_triple, proj_weight):
    image_count, length, feat_width = token_triple.shape
    feature = jnp.dot(
        token_triple.reshape(image_count * length, feat_width),
        proj_weight,
        preferred_element_type=jnp.float32,
    )
    inv_rms = lax.rsqrt(jnp.mean(feature * feature, axis=-1, keepdims=True) + EPSILON)
    normed = feature * inv_rms
    return (normed, inv_rms, normed.astype(jnp.bfloat16).reshape(image_count, length, feat_width))


def edge_terms(first_image_features, second_feats, match_block):
    score_scale = 1.0 / (first_image_features.shape[-1] * SOFTMAX_COOLING)
    scores = (
        jnp.einsum(
            "eid,ejd->eij", first_image_features, second_feats, preferred_element_type=jnp.float32
        )
        * score_scale
    )
    expo = jnp.exp(scores)
    rows = expo / jnp.sum(expo, axis=2, keepdims=True)
    cols = expo / jnp.sum(expo, axis=1, keepdims=True)
    incoming_gradient = match_block.astype(jnp.float32)
    d_rows = incoming_gradient * cols
    d_cols = incoming_gradient * rows
    d_scores = rows * (d_rows - jnp.sum(d_rows * rows, axis=2, keepdims=True)) + cols * (
        d_cols - jnp.sum(d_cols * cols, axis=1, keepdims=True)
    )
    d_scaled = (d_scores * score_scale).astype(jnp.bfloat16)
    grad_first = jnp.einsum(
        "eij,ejd->eid", d_scaled, second_feats, preferred_element_type=jnp.float32
    )
    grad_second = jnp.einsum(
        "eij,eid->ejd", d_scaled, first_image_features, preferred_element_type=jnp.float32
    )
    return (grad_first, grad_second)


def local(tokens, proj_weight, match_grad, edge_first, pair_second_image, send_pick):
    img_count, length, feat_width = tokens.shape
    normed, inv_rms, normed_b = normalize(tokens, proj_weight)
    raw_pool = lax.all_gather(tokens, "sub", axis=0, tiled=True)
    raw_received = lax.all_to_all(
        jnp.take(tokens, send_pick, axis=0), "grp", split_axis=0, concat_axis=0, tiled=True
    )
    pool = normalize(raw_pool, proj_weight)[2]
    received = normalize(raw_received, proj_weight)[2]
    pool_count = pool.shape[0]
    slot_count = received.shape[0]
    edge_count = edge_first.shape[0]
    grads = match_grad.reshape(edge_count, length, length)
    edge_block = 64

    def block_step(block_index, totals):
        pool_total, slot_total = totals
        block_start = block_index * edge_block
        first_images = lax.dynamic_slice_in_dim(edge_first, block_start, edge_block, 0)
        seconds = lax.dynamic_slice_in_dim(pair_second_image, block_start, edge_block, 0)
        block_grads = lax.dynamic_slice_in_dim(grads, block_start, edge_block, 0)
        grad_first, grad_second = edge_terms(
            jnp.take(pool, first_images, axis=0), jnp.take(received, seconds, axis=0), block_grads
        )
        pool_total = pool_total.at[first_images].add(grad_first)
        slot_total = slot_total.at[seconds].add(grad_second)
        return (pool_total, slot_total)

    start_totals = (
        jnp.zeros((pool_count, length, feat_width), jnp.float32),
        jnp.zeros((slot_count, length, feat_width), jnp.float32),
    )
    pool_total, slot_total = lax.fori_loop(0, edge_count // edge_block, block_step, start_totals)
    returned = lax.all_to_all(
        slot_total.astype(jnp.bfloat16), "grp", split_axis=0, concat_axis=0, tiled=True
    )
    owned = lax.psum_scatter(
        pool_total.astype(jnp.bfloat16), "sub", scatter_dimension=0, tiled=True
    ).astype(jnp.float32)
    pick_onehot = (jnp.arange(img_count, dtype=jnp.int32)[:, None] == send_pick[None, :]).astype(
        jnp.bfloat16
    )
    incoming_gradient = owned + jnp.einsum(
        "ir,rld->ild", pick_onehot, returned, preferred_element_type=jnp.float32
    )
    incoming_gradient = incoming_gradient.reshape(img_count * length, feat_width)
    feature_grad = (
        inv_rms
        * (
            incoming_gradient
            - normed * jnp.mean(incoming_gradient * normed, axis=-1, keepdims=True)
        )
    ).astype(jnp.bfloat16)
    token_grad = jnp.einsum(
        "nk,dk->nd", feature_grad, proj_weight, preferred_element_type=jnp.float32
    )
    return token_grad.astype(jnp.bfloat16).reshape(img_count, length, feat_width)


def solution(mesh):
    placed = (
        P(("grp", "sub"), None, None),
        P(),
        P(("grp", "sub"), None),
        P(("grp", "sub")),
        P(("grp", "sub")),
        P(("grp", "sub")),
    )
    return jax.shard_map(
        local, mesh=mesh, in_specs=placed, out_specs=P(("grp", "sub"), None, None), check_vma=False
    )
```

profile of v0, /device:TPU:0, one launch (start us, length us, event | category | flops | bytes accessed | tf_op | source)
XLA Modules:
  0.0 144.9 jit_solution(10182030258065522187)
XLA Ops:
  6.5 0.7 compare_select_fusion.2
  7.3 0.7 compare_and_fusion.2
  7.9 1.4 gather_fusion.2
  9.4 0.9 broadcast_select_fusion.6
  10.3 5.2 %all-to-all-start = ((bf16[32,32,256]{2,1,0:T(8,128)(2,1)}), bf16[32,32,256]{2,1,0:T(8,128)(2,1)S(1)}, u32[]{:S(2)}, u32[]{:S(2)}) async-start(bf16[32,32,256]{2,1,0:T(8,128)(2,1)} %broadcast_select_fusion.6), calls=%async_computation | async-start | bytes 1048576 | tf_op jit(solution)/shard_map/all_to_all | solution.py:53
  15.5 14.2 %all_gather.3 = bf16[16,32,256]{2,1,0:T(8,128)(2,1)S(1)} all-gather(bf16[4,32,256]{2,1,0:T(8,128)(2,1)S(1)} %copy-done.5), channel_id=1, replica_groups=mesh['grp'=8,'sub'=4] {'sub'}, dimensions={0}, use_global_device_ids=true | all-gather | bytes 327680 | tf_op jit(solution)/shard_map/all_gather | solution.py:52
  29.7 0.9 copy.24
  30.6 0.3 multiply_reduce_fusion.3
  30.9 0.1 multiply_convert_fusion.1
  31.1 0.0 all-to-all-done
  31.1 0.0 copy-start.9
  31.1 0.0 copy-start.11
  31.1 0.4 multiply_reduce_fusion.2
  31.5 0.2 multiply_convert_fusion
  31.7 0.1 broadcast_in_dim.81
  31.9 74.0 %while.15 = (s32[]{:T(128)}, f32[16,32,256]{2,1,0:T(8,128)S(1)}, f32[32,32,256]{2,1,0:T(8,128)S(1)}, s32[128]{0:T(128)S(1)}, bf16[16,32,256]{2,1,0:T(8,128)(2,1)...) while((s32[]{:T(128)}, f32[16,32,256]{2,1,0:T(8,128)S(1)}, ...), condition=%wide.region_10.11_spmd, body=%wide.region_3.10_spmd.sunk | while | flops 140456864 | bytes 40517248 | solution.py:81
  32.0 0.0 copy-start.2
  32.0 0.7 compare_and_fusion.4
  32.7 1.6 %gather_fusion = bf16[64,32,256]{2,1,0:T(8,128)(2,1)} fusion(bf16[16,32,256]{2,1,0:T(8,128)(2,1)S(1)} %get-tuple-element.284, s32[1024]{0:T(1024)S(1)} %pad_clamp_fusion.5), kind=kCustom, calls=%fused_computation.clone.1 | custom fusion | bytes 2097408 | tf_op jit(solution)/shard_map/while/body/eval_jaxpr/jit(_take)/gather | solution.py:71
  34.3 0.6 gather_fusion.1
  34.9 0.0 copy-done.2
  34.9 0.0 copy-start.1
  35.0 0.0 copy-start.8
  35.0 3.3 %fusion.59 = f32[64,32,32]{2,1,0:T(8,128)} fusion(bf16[64,32,256]{2,1,0:T(8,128)(2,1)} %gather_fusion, pred[64]{0:T(512)(128)(4,1)} %get-tuple-element.253, bf16[64,32,256]{2,1,0:T(8,128)(2,1)S(1)} %gather_fusion.1, pred[64]{0:T(512)(128)(4,1)S(1)} %get-tuple-element.255), kind=kOutput, calls=%fused_computation.9.clone.1 | convolution fusion | flops 34736160 | bytes 2359424 | tf_op jit(solution)/shard_map/while/body/eval_jaxpr/div | solution.py:31
  38.2 0.0 copy-done.8
  38.2 2.8 %fusion.58 = f32[64,32,32]{2,1,0:T(8,128)} fusion(bf16[64,32,256]{2,1,0:T(8,128)(2,1)} %gather_fusion, pred[64]{0:T(512)(128)(4,1)S(1)} %copy-done.8, bf16[64,32,256]{2,1,0:T(8,128)(2,1)S(1)} %gather_fusion.1, pred[64]{0:T(512)(128)(4,1)S(1)} %get-tuple-element.255), kind=kOutput, calls=%fused_computation.10.clone.1 | convolution fusion | flops 34736160 | bytes 2359424 | tf_op jit(solution)/shard_map/while/body/eval_jaxpr/div | solution.py:32
  41.1 0.0 copy-done.4
  41.1 0.1 constant_dynamic-slice_fusion.2
  41.2 0.8 copy.34
  42.0 2.5 %fusion.60 = f32[64,32,32]{2,1,0:T(8,128)S(1)} fusion(f32[64,32,32]{2,1,0:T(8,128)} %fusion.58, f32[64,32,32]{2,1,0:T(8,128)} %fusion.59, bf16[64,32,32]{2,1,0:T(8,128)(2,1)S(1)} %copy.34), kind=kOutput, calls=%fused_computation.16.clone.1 | output fusion | flops 460831 | bytes 917504 | tf_op jit(solution)/shard_map/while/body/eval_jaxpr/sub | solution.py:37
  44.5 5.0 %fusion.62 = f32[64,32,256]{2,1,0:T(8,128)} fusion(f32[64,32,32]{2,1,0:T(8,128)S(1)} %fusion.60, f32[64,32,32]{2,1,0:T(8,128)} %fusion.59, bf16[64,32,256]{2,1,0:T(8,128)(2,1)} %gather_fusion, pred[64]{0:T(512)(128)(4,1)S(1)} %copy-done.8, f32[64,32,32]{2,1,0:T(8,128)} %fusion.58, bf16[64,32,32]{2,1,0:T(8,128)(2,1)S(1)} %copy.34), kind=kOutput, calls=%fused_computation.28.clone.1 | convolution fusion | flops 34736160 | bytes 4063296 | tf_op jit(solution)/shard_map/while/body/eval_jaxpr/eij,eid->ejd/dot_general | solution.py:43
  49.5 7.0 %scatter_fusion.1 = f32[32,32,256]{2,1,0:T(8,128)S(1)} fusion(f32[32,32,256]{2,1,0:T(8,128)S(1)} %get-tuple-element.270, s32[64]{0:T(128)S(1)} %get-tuple-element.254, f32[64,32,256]{2,1,0:T(8,128)} %fusion.62), kind=kCustom, calls=%fused_computation.4.clone.1 | custom fusion | flops 524288 | bytes 6291712 | tf_op jit(solution)/shard_map/while/body/eval_jaxpr/scatter-add | solution.py:74
  56.6 5.3 %fusion.61 = f32[64,32,256]{2,1,0:T(8,128)} fusion(f32[64,32,32]{2,1,0:T(8,128)S(1)} %fusion.60, f32[64,32,32]{2,1,0:T(8,128)} %fusion.59, bf16[64,32,256]{2,1,0:T(8,128)(2,1)} %copy-done.1, pred[64]{0:T(512)(128)(4,1)S(1)} %get-tuple-element.255, f32[64,32,32]{2,1,0:T(8,128)} %fusion.58, bf16[64,32,32]{2,1,0:T(8,128)(2,1)S(1)} %copy.34), kind=kOutput, calls=%fused_computation.29.clone.1 | convolution fusion | flops 34736160 | bytes 4063296 | tf_op jit(solution)/shard_map/while/body/eval_jaxpr/eij,ejd->eid/dot_general | solution.py:40
  61.9 7.0 %scatter_fusion = f32[16,32,256]{2,1,0:T(8,128)S(1)} fusion(f32[16,32,256]{2,1,0:T(8,128)S(1)} %get-tuple-element.269, s32[64]{0:T(128)S(1)} %get-tuple-element.252, f32[64,32,256]{2,1,0:T(8,128)} %fusion.61), kind=kCustom, calls=%fused_computation.3.clone.1 | custom fusion | flops 524288 | bytes 6291712 | tf_op jit(solution)/shard_map/while/body/eval_jaxpr/scatter-add | solution.py:73
  68.9 0.0 copy-done.3
  68.9 0.0 copy-done.10
  68.9 0.0 copy-done.12
  69.0 0.7 compare_and_fusion.4
  69.7 1.6 %gather_fusion = bf16[64,32,256]{2,1,0:T(8,128)(2,1)} fusion(bf16[16,32,256]{2,1,0:T(8,128)(2,1)S(1)} %get-tuple-element.284, s32[1024]{0:T(1024)S(1)} %pad_clamp_fusion.5), kind=kCustom, calls=%fused_computation.clone.1 | custom fusion | bytes 2097408 | tf_op jit(solution)/shard_map/while/body/eval_jaxpr/jit(_take)/gather | solution.py:71
  71.3 0.6 gather_fusion.1
  71.9 3.3 %fusion.59 = f32[64,32,32]{2,1,0:T(8,128)} fusion(bf16[64,32,256]{2,1,0:T(8,128)(2,1)} %gather_fusion, pred[64]{0:T(512)(128)(4,1)} %get-tuple-element.253, bf16[64,32,256]{2,1,0:T(8,128)(2,1)S(1)} %gather_fusion.1, pred[64]{0:T(512)(128)(4,1)S(1)} %get-tuple-element.255), kind=kOutput, calls=%fused_computation.9.clone.1 | convolution fusion | flops 34736160 | bytes 2359424 | tf_op jit(solution)/shard_map/while/body/eval_jaxpr/div | solution.py:31
  75.2 2.8 %fusion.58 = f32[64,32,32]{2,1,0:T(8,128)} fusion(bf16[64,32,256]{2,1,0:T(8,128)(2,1)} %gather_fusion, pred[64]{0:T(512)(128)(4,1)S(1)} %copy-done.8, bf16[64,32,256]{2,1,0:T(8,128)(2,1)S(1)} %gather_fusion.1, pred[64]{0:T(512)(128)(4,1)S(1)} %get-tuple-element.255), kind=kOutput, calls=%fused_computation.10.clone.1 | convolution fusion | flops 34736160 | bytes 2359424 | tf_op jit(solution)/shard_map/while/body/eval_jaxpr/div | solution.py:32
  78.1 0.1 constant_dynamic-slice_fusion.2
  78.2 0.8 copy.34
  79.0 2.5 %fusion.60 = f32[64,32,32]{2,1,0:T(8,128)S(1)} fusion(f32[64,32,32]{2,1,0:T(8,128)} %fusion.58, f32[64,32,32]{2,1,0:T(8,128)} %fusion.59, bf16[64,32,32]{2,1,0:T(8,128)(2,1)S(1)} %copy.34), kind=kOutput, calls=%fused_computation.16.clone.1 | output fusion | flops 460831 | bytes 917504 | tf_op jit(solution)/shard_map/while/body/eval_jaxpr/sub | solution.py:37
  81.5 5.0 %fusion.62 = f32[64,32,256]{2,1,0:T(8,128)} fusion(f32[64,32,32]{2,1,0:T(8,128)S(1)} %fusion.60, f32[64,32,32]{2,1,0:T(8,128)} %fusion.59, bf16[64,32,256]{2,1,0:T(8,128)(2,1)} %gather_fusion, pred[64]{0:T(512)(128)(4,1)S(1)} %copy-done.8, f32[64,32,32]{2,1,0:T(8,128)} %fusion.58, bf16[64,32,32]{2,1,0:T(8,128)(2,1)S(1)} %copy.34), kind=kOutput, calls=%fused_computation.28.clone.1 | convolution fusion | flops 34736160 | bytes 4063296 | tf_op jit(solution)/shard_map/while/body/eval_jaxpr/eij,eid->ejd/dot_general | solution.py:43
  86.5 7.0 %scatter_fusion.1 = f32[32,32,256]{2,1,0:T(8,128)S(1)} fusion(f32[32,32,256]{2,1,0:T(8,128)S(1)} %get-tuple-element.270, s32[64]{0:T(128)S(1)} %get-tuple-element.254, f32[64,32,256]{2,1,0:T(8,128)} %fusion.62), kind=kCustom, calls=%fused_computation.4.clone.1 | custom fusion | flops 524288 | bytes 6291712 | tf_op jit(solution)/shard_map/while/body/eval_jaxpr/scatter-add | solution.py:74
  93.6 5.3 %fusion.61 = f32[64,32,256]{2,1,0:T(8,128)} fusion(f32[64,32,32]{2,1,0:T(8,128)S(1)} %fusion.60, f32[64,32,32]{2,1,0:T(8,128)} %fusion.59, bf16[64,32,256]{2,1,0:T(8,128)(2,1)} %copy-done.1, pred[64]{0:T(512)(128)(4,1)S(1)} %get-tuple-element.255, f32[64,32,32]{2,1,0:T(8,128)} %fusion.58, bf16[64,32,32]{2,1,0:T(8,128)(2,1)S(1)} %copy.34), kind=kOutput, calls=%fused_computation.29.clone.1 | convolution fusion | flops 34736160 | bytes 4063296 | tf_op jit(solution)/shard_map/while/body/eval_jaxpr/eij,ejd->eid/dot_general | solution.py:40
  98.9 7.0 %scatter_fusion = f32[16,32,256]{2,1,0:T(8,128)S(1)} fusion(f32[16,32,256]{2,1,0:T(8,128)S(1)} %get-tuple-element.269, s32[64]{0:T(128)S(1)} %get-tuple-element.252, f32[64,32,256]{2,1,0:T(8,128)} %fusion.61), kind=kCustom, calls=%fused_computation.3.clone.1 | custom fusion | flops 524288 | bytes 6291712 | tf_op jit(solution)/shard_map/while/body/eval_jaxpr/scatter-add | solution.py:73
  105.9 0.0 copy-start.6
  106.0 0.0 copy-start.13
  106.0 0.9 convert_element_type.40
  106.8 4.0 %all-to-all-start.1 = ((bf16[32,32,256]{2,1,0:T(8,128)(2,1)}), bf16[32,32,256]{2,1,0:T(8,128)(2,1)S(1)}, u32[]{:S(2)}, u32[]{:S(2)}) async-start(bf16[32,32,256]{2,1,0:T(8,128)(2,1)} %convert_element_type.40), calls=%async_computation.2 | async-start | bytes 1048576 | tf_op jit(solution)/shard_map/all_to_all | solution.py:82
  110.9 0.0 reduce-scatter.2.cloned.1.call-start
  110.9 0.7 convert_element_type.38
  111.7 0.0 reduce-scatter.2.cloned.1.call-update
  111.7 0.3 multiply_reduce_fusion.4
  112.0 8.6 %all-to-all-done.1 = bf16[32,32,256]{2,1,0:T(8,128)(2,1)S(1)} async-done(((bf16[32,32,256]{2,1,0:T(8,128)(2,1)}), bf16[32,32,256]{2,1,0:T(8,128)(2,1)S(1)}, u32[]{:S(2)}, u32[]{:S(2)}) %all-to-all-start.1) | async-done | bytes 524320 | tf_op jit(solution)/shard_map/all_to_all | solution.py:82
  120.6 0.4 fusion.31
  121.0 15.0 %reduce-scatter.2.cloned.1.call-done = bf16[4,32,256]{2,1,0:T(8,128)(2,1)} async-done(((bf16[16,32,256]{2,1,0:T(8,128)(2,1)}), bf16[4,32,256]{2,1,0:T(8,128)(2,1)}) %reduce-scatter.2.cloned.1.call-update) | async-done | bytes 65552 | tf_op jit(solution)/shard_map/reduce_scatter | solution.py:85
  136.0 0.9 copy_add_fusion
  136.9 0.2 fusion.33
  137.1 0.1 fusion.35
  137.2 0.8 convolution_convert_fusion
  (39 shorter events, 0.2 us)
Async XLA Ops:
  6.5 24.0 %copy-start = (bf16[256,256]{1,0:T(8,128)(2,1)S(1)}, bf16[256,256]{1,0:T(8,128)(2,1)}, u32[]{:S(2)}) copy-start(bf16[256,256]{1,0:T(8,128)(2,1)} %param.9) | copy-start | bytes 393220
  6.5 8.9 %copy-start.5 = (bf16[4,32,256]{2,1,0:T(8,128)(2,1)S(1)}, bf16[4,32,256]{2,1,0:T(8,128)(2,1)}, u32[]{:S(2)}) copy-start(bf16[4,32,256]{2,1,0:T(8,128)(2,1)} %param.8) | copy-start | bytes 196612
  6.5 23.2 %copy-start.7 = (bf16[128,1024]{1,0:T(8,128)(2,1)S(1)}, bf16[128,1024]{1,0:T(8,128)(2,1)}, u32[]{:S(2)}) copy-start(bf16[128,1024]{1,0:T(8,128)(2,1)} %param.10) | copy-start | bytes 786436
  10.3 20.8 %all-to-all-start = ((bf16[32,32,256]{2,1,0:T(8,128)(2,1)}), bf16[32,32,256]{2,1,0:T(8,128)(2,1)S(1)}, u32[]{:S(2)}, u32[]{:S(2)}) async-start(bf16[32,32,256]{2,1,0:T(8,128)(2,1)} %broadcast_select_fusion.6), calls=%async_computation | async-start | bytes 1048576 | tf_op jit(solution)/shard_map/all_to_all | solution.py:53
  31.1 0.8 copy-start.9
  31.1 0.8 copy-start.11
  32.0 3.0 %copy-start.2 = (bf16[32,32,256]{2,1,0:T(8,128)(2,1)}, bf16[32,32,256]{2,1,0:T(8,128)(2,1)S(1)}, u32[]{:S(2)}) copy-start(bf16[32,32,256]{2,1,0:T(8,128)(2,1)S(1)} %get-tuple-element.286) | copy-start | bytes 1572868 | tf_op jit(solution)/shard_map/while
  34.9 3.3 %copy-start.1 = (bf16[64,32,256]{2,1,0:T(8,128)(2,1)}, bf16[64,32,256]{2,1,0:T(8,128)(2,1)S(1)}, u32[]{:S(2)}) copy-start(bf16[64,32,256]{2,1,0:T(8,128)(2,1)S(1)} %gather_fusion.1) | copy-start | bytes 3145732 | tf_op jit(solution)/shard_map/while
  35.0 3.3 %copy-start.8 = (pred[64]{0:T(512)(128)(4,1)S(1)}, pred[64]{0:T(512)(128)(4,1)}, u32[]{:S(2)}) copy-start(pred[64]{0:T(512)(128)(4,1)} %get-tuple-element.253) | copy-start | bytes 196 | tf_op jit(solution)/shard_map/while
  38.2 2.9 %copy-start.4 = (bf16[128,32,32]{0,2,1:T(8,128)(2,1)S(1)}, bf16[128,32,32]{0,2,1:T(8,128)(2,1)}, u32[]{:S(2)}) copy-start(bf16[128,32,32]{0,2,1:T(8,128)(2,1)} %get-tuple-element.287) | copy-start | bytes 786436 | tf_op jit(solution)/shard_map/while
  61.9 7.0 %copy-start.3 = (bf16[32,32,256]{2,1,0:T(8,128)(2,1)S(1)}, bf16[32,32,256]{2,1,0:T(8,128)(2,1)}, u32[]{:S(2)}) copy-start(bf16[32,32,256]{2,1,0:T(8,128)(2,1)} %copy-done.2) | copy-start | bytes 1572868 | tf_op jit(solution)/shard_map/while
  61.9 7.0 %copy-start.10 = (s32[128]{0:T(128)S(1)}, s32[128]{0:T(128)}, u32[]{:S(2)}) copy-start(s32[128]{0:T(128)} %get-tuple-element.310) | copy-start | bytes 1540 | tf_op jit(solution)/shard_map/while
  61.9 7.1 %copy-start.12 = (s32[128]{0:T(128)S(1)}, s32[128]{0:T(128)}, u32[]{:S(2)}) copy-start(s32[128]{0:T(128)} %get-tuple-element.324) | copy-start | bytes 1540 | tf_op jit(solution)/shard_map/while
  68.9 3.0 %copy-start.2 = (bf16[32,32,256]{2,1,0:T(8,128)(2,1)}, bf16[32,32,256]{2,1,0:T(8,128)(2,1)S(1)}, u32[]{:S(2)}) copy-start(bf16[32,32,256]{2,1,0:T(8,128)(2,1)S(1)} %get-tuple-element.286) | copy-start | bytes 1572868 | tf_op jit(solution)/shard_map/while
  71.9 3.3 %copy-start.1 = (bf16[64,32,256]{2,1,0:T(8,128)(2,1)}, bf16[64,32,256]{2,1,0:T(8,128)(2,1)S(1)}, u32[]{:S(2)}) copy-start(bf16[64,32,256]{2,1,0:T(8,128)(2,1)S(1)} %gather_fusion.1) | copy-start | bytes 3145732 | tf_op jit(solution)/shard_map/while
  71.9 3.3 %copy-start.8 = (pred[64]{0:T(512)(128)(4,1)S(1)}, pred[64]{0:T(512)(128)(4,1)}, u32[]{:S(2)}) copy-start(pred[64]{0:T(512)(128)(4,1)} %get-tuple-element.253) | copy-start | bytes 196 | tf_op jit(solution)/shard_map/while
  75.2 2.9 %copy-start.4 = (bf16[128,32,32]{0,2,1:T(8,128)(2,1)S(1)}, bf16[128,32,32]{0,2,1:T(8,128)(2,1)}, u32[]{:S(2)}) copy-start(bf16[128,32,32]{0,2,1:T(8,128)(2,1)} %get-tuple-element.287) | copy-start | bytes 786436 | tf_op jit(solution)/shard_map/while
  98.9 7.0 %copy-start.3 = (bf16[32,32,256]{2,1,0:T(8,128)(2,1)S(1)}, bf16[32,32,256]{2,1,0:T(8,128)(2,1)}, u32[]{:S(2)}) copy-start(bf16[32,32,256]{2,1,0:T(8,128)(2,1)} %copy-done.2) | copy-start | bytes 1572868 | tf_op jit(solution)/shard_map/while
  98.9 7.1 %copy-start.10 = (s32[128]{0:T(128)S(1)}, s32[128]{0:T(128)}, u32[]{:S(2)}) copy-start(s32[128]{0:T(128)} %get-tuple-element.310) | copy-start | bytes 1540 | tf_op jit(solution)/shard_map/while
  98.9 7.1 %copy-start.12 = (s32[128]{0:T(128)S(1)}, s32[128]{0:T(128)}, u32[]{:S(2)}) copy-start(s32[128]{0:T(128)} %get-tuple-element.324) | copy-start | bytes 1540 | tf_op jit(solution)/shard_map/while
  105.9 5.7 %copy-start.6 = (bf16[4,32,256]{2,1,0:T(8,128)(2,1)S(1)}, bf16[4,32,256]{2,1,0:T(8,128)(2,1)}, u32[]{:S(2)}) copy-start(bf16[4,32,256]{2,1,0:T(8,128)(2,1)} %param.8) | copy-start | bytes 196612
  106.0 14.6 %copy-start.13 = (s32[32]{0:T(128)S(1)}, s32[32]{0:T(128)}, u32[]{:S(2)}) copy-start(s32[32]{0:T(128)} %param.13) | copy-start | bytes 388
  106.8 13.7 %all-to-all-start.1 = ((bf16[32,32,256]{2,1,0:T(8,128)(2,1)}), bf16[32,32,256]{2,1,0:T(8,128)(2,1)S(1)}, u32[]{:S(2)}, u32[]{:S(2)}) async-start(bf16[32,32,256]{2,1,0:T(8,128)(2,1)} %convert_element_type.40), calls=%async_computation.2 | async-start | bytes 1048576 | tf_op jit(solution)/shard_map/all_to_all | solution.py:82
  110.9 25.2 %reduce-scatter.2.cloned.1.call-start = ((), (), s32[]{:S(2)}) async-start(), calls=%async_computation.3 | async-start | bytes 327680 | tf_op jit(solution)/shard_map/reduce_scatter | solution.py:85
Sparse Core Ops, SparseCore 0:
  113.9 22.0 reduce-scatter.1
where the time goes:
time: 146 us; the launch traced here: 145 us
  other arithmetic  40 us (27%)
  matrix products  35 us (24%)
  waiting for transfers between devices  23.7 us (16%)
  blocking collectives  14.2 us (10%)
  between operations  13.6 us (9%)
  starting transfers between devices  9.27 us (6%)
  local copies, waits for them, and re-layouts  8.82 us (6%)
    reduce_scatter x1, waiting for transfers between devices, local(): lax.psum_scatter(pool_total.astype(jnp.bfloat16), 'sub', scatter_dimensio...  15 us
    all_gather x1, blocking collectives, local(): raw_pool = lax.all_gather(tokens, 'sub', axis=0, tiled=True)  14.2 us
    scatter-add x2, other arithmetic, block_step(): slot_total = slot_total.at[seconds].add(grad_second)  14.1 us
    scatter-add x2, other arithmetic, block_step(): pool_total = pool_total.at[first_images].add(grad_first)  14 us
    dot_general x2, matrix products, edge_terms(): jnp.einsum('eij,ejd->eid', d_scaled, second_feats, preferred_element_type...  10.6 us
    dot_general x2, matrix products, edge_terms(): jnp.einsum('eij,eid->ejd', d_scaled, first_image_features, preferred_elem...  10 us
    all_to_all x1, waiting for transfers between devices, local(): lax.all_to_all(slot_total.astype(jnp.bfloat16), 'grp', split_axis=0, conc...  8.62 us
    div x2, matrix products, edge_terms(): rows = expo / jnp.sum(expo, axis=2, keepdims=True)  6.51 us
  transfers between devices with their start and end apart: 3, of which 2 were waited for; matrix products, arithmetic and copies ran while one was open for 2% of the time, Pallas kernels for 0%

commit v1 on v0

--- a/solution.py
+++ b/solution.py
@@ -5,6 +5,12 @@
 
 EPSILON = 1e-05
 SOFTMAX_COOLING = 0.1
+
+
+def in_order(tiles, dim):
+    shape = list(tiles.shape[1:])
+    shape[dim] *= tiles.shape[0]
+    return jnp.moveaxis(tiles, 0, dim).reshape(shape)
 
 
 def normalize(token_triple, proj_weight):
@@ -49,7 +55,19 @@
 def local(tokens, proj_weight, match_grad, edge_first, pair_second_image, send_pick):
     img_count, length, feat_width = tokens.shape
     normed, inv_rms, normed_b = normalize(tokens, proj_weight)
-    raw_pool = lax.all_gather(tokens, "sub", axis=0, tiled=True)
+    peers = lax.axis_size("sub")
+    pairs = [(i, (i + 1) % peers) for i in range(peers)]
+    back = [(b, a) for a, b in pairs]
+    lower, upper = ([], [])
+    for step in range(peers - 1):
+        if step % 2 == 0:
+            lower.append(lax.ppermute(lower[-1] if lower else tokens, "sub", pairs))
+        else:
+            upper.append(lax.ppermute(upper[-1] if upper else tokens, "sub", back))
+    blocks = jnp.stack([*lower[::-1], tokens, *upper])
+    shift = lax.axis_index("sub") - len(lower)
+    blocks = blocks[(jnp.arange(peers) - shift) % peers]
+    raw_pool = in_order(blocks, 0)
     raw_received = lax.all_to_all(
         jnp.take(tokens, send_pick, axis=0), "grp", split_axis=0, concat_axis=0, tiled=True
     )

time: 146 us -> 141 us (0.966)
  blocking collectives: 14.2 us -> 0 us
  waiting for transfers between devices: 23.7 us -> 29.1 us
  starting transfers between devices: 9.27 us -> 12.6 us
    all_gather x1 -> x0, blocking collectives: 14.2 us -> none  [local(): raw_pool = lax.all_gather(tokens, 'sub', axis=0, tiled=True)]
    ppermute x0 -> x3, waiting for transfers between devices: none -> 6.26 us  [the longest x2 6.26 us: local(): lower.append(lax.ppermute(lower[-1] if lower else tokens, 'sub', pairs))]
    ppermute x0 -> x3, starting transfers between devices: none -> 5.19 us  [the longest x2 3.11 us: local(): lower.append(lax.ppermute(lower[-1] if lower else tokens, 'sub', pairs))]
    reduce_scatter x1, waiting for transfers between devices: 15 us -> 12.9 us  [local(): lax.psum_scatter(pool_total.astype(jnp.bfloat16), 'sub', scatter_dimensio...]
  transfers between devices with their start and end apart: 3 -> 6, of which waited for: 2 -> 4; matrix products, arithmetic and copies ran while one was open for 2% -> 5% of each run, Pallas kernels for 0% -> 0%
where the time goes in v1:
time: 141 us; the launch traced here: 140 us
  other arithmetic  40 us (28%)
  matrix products  35 us (25%)
  waiting for transfers between devices  29.1 us (21%)
  between operations  13.6 us (10%)
  starting transfers between devices  12.6 us (9%)
  local copies, waits for them, and re-layouts  9.38 us (7%)
    scatter-add x2, other arithmetic, block_step(): slot_total = slot_total.at[seconds].add(grad_second)  14.1 us
    scatter-add x2, other arithmetic, block_step(): pool_total = pool_total.at[first_images].add(grad_first)  14 us
    reduce_scatter x1, waiting for transfers between devices, local(): lax.psum_scatter(pool_total.astype(jnp.bfloat16), 'sub', scatter_dimensio...  12.9 us
    dot_general x2, matrix products, edge_terms(): jnp.einsum('eij,ejd->eid', d_scaled, second_feats, preferred_element_type...  10.6 us
    dot_general x2, matrix products, edge_terms(): jnp.einsum('eij,eid->ejd', d_scaled, first_image_features, preferred_elem...  10 us
    all_to_all x1, waiting for transfers between devices, local(): lax.all_to_all(slot_total.astype(jnp.bfloat16), 'grp', split_axis=0, conc...  8.55 us
    div x2, matrix products, edge_terms(): rows = expo / jnp.sum(expo, axis=2, keepdims=True)  6.51 us
    ppermute x2, waiting for transfers between devices, local(): lower.append(lax.ppermute(lower[-1] if lower else tokens, 'sub', pairs))  6.26 us
  transfers between devices with their start and end apart: 6, of which 4 were waited for; matrix products, arithmetic and copies ran while one was open for 5% of the time, Pallas kernels for 0%

profile of v1, /device:TPU:0, one launch (start us, length us, event | category | flops | bytes accessed | tf_op | source)
XLA Modules:
  0.0 139.9 jit_solution(4873073892565318043)
XLA Ops:
  6.5 3.1 %collective-permute-start = (bf16[4,32,256]{2,1,0:T(8,128)(2,1)}, bf16[4,32,256]{2,1,0:T(8,128)(2,1)S(1)}, u32[]{:S(2)}, u32[]{:S(2)}) collective-permute-start(bf16[4,32,256]{2,1,0:T(8,128)(2,1)} %param.8), channel_id=1, source_target_pairs={{0,1},{1,2},{2,3},{3,0},{4,5},{5,6},{6,7},{7,4},{8,9},{9,10},{10,1... | collective-permute-start | bytes 196616 | tf_op jit(solution)/shard_map/ppermute | solution.py:64
  9.6 2.1 %collective-permute-start.2 = (bf16[4,32,256]{2,1,0:T(8,128)(2,1)}, bf16[4,32,256]{2,1,0:T(8,128)(2,1)S(1)}, u32[]{:S(2)}, u32[]{:S(2)}) collective-permute-start(bf16[4,32,256]{2,1,0:T(8,128)(2,1)} %param.8), channel_id=1, source_target_pairs={{1,0},{2,1},{3,2},{0,3},{5,4},{6,5},{7,6},{4,7},{9,8},{10,9},{11,1... | collective-permute-start | bytes 196616 | tf_op jit(solution)/shard_map/ppermute | solution.py:66
  11.7 0.7 compare_select_fusion.2
  12.3 0.7 compare_and_fusion.2
  13.0 1.4 %gather_fusion.3 = bf16[32,32,256]{2,1,0:T(8,128)(2,1)S(1)} fusion(bf16[4,32,256]{2,1,0:T(8,128)(2,1)} %param.8, s32[1024]{0:T(1024)S(1)} %pad_clamp_fusion.2), kind=kCustom, calls=%fused_computation.3 | custom fusion | bytes 1048704 | tf_op jit(solution)/shard_map/jit(_take)/gather | solution.py:72
  14.4 0.9 broadcast_select_fusion.6
  15.3 3.9 %all-to-all-start = ((bf16[32,32,256]{2,1,0:T(8,128)(2,1)}), bf16[32,32,256]{2,1,0:T(8,128)(2,1)S(1)}, u32[]{:S(2)}, u32[]{:S(2)}) async-start(bf16[32,32,256]{2,1,0:T(8,128)(2,1)} %broadcast_select_fusion.6), calls=%async_computation | async-start | bytes 1048576 | tf_op jit(solution)/shard_map/all_to_all | solution.py:71
  19.2 0.9 copy.24
  20.1 0.0 collective-permute-done
  20.1 0.1 collective-permute-start.1
  20.2 0.0 collective-permute-done.2
  20.2 6.3 %collective-permute-done.1 = bf16[4,32,256]{2,1,0:T(8,128)(2,1)S(1)} collective-permute-done((bf16[4,32,256]{2,1,0:T(8,128)(2,1)S(1)}, bf16[4,32,256]{2,1,0:T(8,128)(2,1)S(1)}, u32[]{:S(2)}, u32[]{:S(2)}) %collective-permute-start.1) | collective-permute-done | bytes 65568 | tf_op jit(solution)/shard_map/ppermute | solution.py:64
  26.5 0.6 gather_fusion.2
  27.1 0.0 copy-done
  27.1 0.3 multiply_reduce_fusion.3
  27.4 0.1 multiply_convert_fusion.1
  27.6 1.3 all-to-all-done
  28.9 0.4 multiply_reduce_fusion.2
  29.4 0.2 multiply_convert_fusion
  29.6 0.1 broadcast_in_dim.82
  29.7 0.0 copy-done.9
  29.8 0.0 copy-done.11
  29.8 74.0 %while.15 = (s32[]{:T(128)}, f32[16,32,256]{2,1,0:T(8,128)S(1)}, f32[32,32,256]{2,1,0:T(8,128)S(1)}, s32[128]{0:T(128)S(1)}, bf16[16,32,256]{2,1,0:T(8,128)(2,1)...) while((s32[]{:T(128)}, f32[16,32,256]{2,1,0:T(8,128)S(1)}, ...), condition=%wide.region_10.11_spmd, body=%wide.region_3.10_spmd.sunk | while | flops 140456864 | bytes 40517248 | solution.py:99
  29.8 0.7 compare_and_fusion.4
  30.5 1.6 %gather_fusion = bf16[64,32,256]{2,1,0:T(8,128)(2,1)} fusion(bf16[16,32,256]{2,1,0:T(8,128)(2,1)S(1)} %get-tuple-element.284, s32[1024]{0:T(1024)S(1)} %pad_clamp_fusion.6), kind=kCustom, calls=%fused_computation.clone.1 | custom fusion | bytes 2097408 | tf_op jit(solution)/shard_map/while/body/eval_jaxpr/jit(_take)/gather | solution.py:89
  32.1 0.6 gather_fusion.1
  32.8 3.3 %fusion.61 = f32[64,32,32]{2,1,0:T(8,128)} fusion(bf16[64,32,256]{2,1,0:T(8,128)(2,1)} %gather_fusion, pred[64]{0:T(512)(128)(4,1)} %get-tuple-element.253, bf16[64,32,256]{2,1,0:T(8,128)(2,1)S(1)} %gather_fusion.1, pred[64]{0:T(512)(128)(4,1)S(1)} %get-tuple-element.255), kind=kOutput, calls=%fused_computation.10.clone.1 | convolution fusion | flops 34736160 | bytes 2359424 | tf_op jit(solution)/shard_map/while/body/eval_jaxpr/div | solution.py:37
  36.1 2.8 %fusion.60 = f32[64,32,32]{2,1,0:T(8,128)} fusion(bf16[64,32,256]{2,1,0:T(8,128)(2,1)} %gather_fusion, pred[64]{0:T(512)(128)(4,1)S(1)} %copy-done.8, bf16[64,32,256]{2,1,0:T(8,128)(2,1)S(1)} %gather_fusion.1, pred[64]{0:T(512)(128)(4,1)S(1)} %get-tuple-element.255), kind=kOutput, calls=%fused_computation.11.clone.1 | convolution fusion | flops 34736160 | bytes 2359424 | tf_op jit(solution)/shard_map/while/body/eval_jaxpr/div | solution.py:38
  38.9 0.1 constant_dynamic-slice_fusion.2
  39.0 0.8 copy.34
  39.8 2.5 %fusion.62 = f32[64,32,32]{2,1,0:T(8,128)S(1)} fusion(f32[64,32,32]{2,1,0:T(8,128)} %fusion.60, f32[64,32,32]{2,1,0:T(8,128)} %fusion.61, bf16[64,32,32]{2,1,0:T(8,128)(2,1)S(1)} %copy.34), kind=kOutput, calls=%fused_computation.17.clone.1 | output fusion | flops 460831 | bytes 917504 | tf_op jit(solution)/shard_map/while/body/eval_jaxpr/sub | solution.py:43
  42.3 5.0 %fusion.64 = f32[64,32,256]{2,1,0:T(8,128)} fusion(f32[64,32,32]{2,1,0:T(8,128)S(1)} %fusion.62, f32[64,32,32]{2,1,0:T(8,128)} %fusion.61, bf16[64,32,256]{2,1,0:T(8,128)(2,1)} %gather_fusion, pred[64]{0:T(512)(128)(4,1)S(1)} %copy-done.8, f32[64,32,32]{2,1,0:T(8,128)} %fusion.60, bf16[64,32,32]{2,1,0:T(8,128)(2,1)S(1)} %copy.34), kind=kOutput, calls=%fused_computation.29.clone.1 | convolution fusion | flops 34736160 | bytes 4063296 | tf_op jit(solution)/shard_map/while/body/eval_jaxpr/eij,eid->ejd/dot_general | solution.py:49
  47.4 7.0 %scatter_fusion.1 = f32[32,32,256]{2,1,0:T(8,128)S(1)} fusion(f32[32,32,256]{2,1,0:T(8,128)S(1)} %get-tuple-element.270, s32[64]{0:T(128)S(1)} %get-tuple-element.254, f32[64,32,256]{2,1,0:T(8,128)} %fusion.64), kind=kCustom, calls=%fused_computation.5.clone.1 | custom fusion | flops 524288 | bytes 6291712 | tf_op jit(solution)/shard_map/while/body/eval_jaxpr/scatter-add | solution.py:92
  54.4 5.3 %fusion.63 = f32[64,32,256]{2,1,0:T(8,128)} fusion(f32[64,32,32]{2,1,0:T(8,128)S(1)} %fusion.62, f32[64,32,32]{2,1,0:T(8,128)} %fusion.61, bf16[64,32,256]{2,1,0:T(8,128)(2,1)} %copy-done.1, pred[64]{0:T(512)(128)(4,1)S(1)} %get-tuple-element.255, f32[64,32,32]{2,1,0:T(8,128)} %fusion.60, bf16[64,32,32]{2,1,0:T(8,128)(2,1)S(1)} %copy.34), kind=kOutput, calls=%fused_computation.30.clone.1 | convolution fusion | flops 34736160 | bytes 4063296 | tf_op jit(solution)/shard_map/while/body/eval_jaxpr/eij,ejd->eid/dot_general | solution.py:46
  59.7 7.0 %scatter_fusion = f32[16,32,256]{2,1,0:T(8,128)S(1)} fusion(f32[16,32,256]{2,1,0:T(8,128)S(1)} %get-tuple-element.269, s32[64]{0:T(128)S(1)} %get-tuple-element.252, f32[64,32,256]{2,1,0:T(8,128)} %fusion.63), kind=kCustom, calls=%fused_computation.4.clone.1 | custom fusion | flops 524288 | bytes 6291712 | tf_op jit(solution)/shard_map/while/body/eval_jaxpr/scatter-add | solution.py:91
  66.8 0.0 copy-start.2
  66.8 0.7 compare_and_fusion.4
  67.5 1.6 %gather_fusion = bf16[64,32,256]{2,1,0:T(8,128)(2,1)} fusion(bf16[16,32,256]{2,1,0:T(8,128)(2,1)S(1)} %get-tuple-element.284, s32[1024]{0:T(1024)S(1)} %pad_clamp_fusion.6), kind=kCustom, calls=%fused_computation.clone.1 | custom fusion | bytes 2097408 | tf_op jit(solution)/shard_map/while/body/eval_jaxpr/jit(_take)/gather | solution.py:89
  69.1 0.6 gather_fusion.1
  69.7 0.0 copy-done.2
  69.8 3.3 %fusion.61 = f32[64,32,32]{2,1,0:T(8,128)} fusion(bf16[64,32,256]{2,1,0:T(8,128)(2,1)} %gather_fusion, pred[64]{0:T(512)(128)(4,1)} %get-tuple-element.253, bf16[64,32,256]{2,1,0:T(8,128)(2,1)S(1)} %gather_fusion.1, pred[64]{0:T(512)(128)(4,1)S(1)} %get-tuple-element.255), kind=kOutput, calls=%fused_computation.10.clone.1 | convolution fusion | flops 34736160 | bytes 2359424 | tf_op jit(solution)/shard_map/while/body/eval_jaxpr/div | solution.py:37
  73.0 2.8 %fusion.60 = f32[64,32,32]{2,1,0:T(8,128)} fusion(bf16[64,32,256]{2,1,0:T(8,128)(2,1)} %gather_fusion, pred[64]{0:T(512)(128)(4,1)S(1)} %copy-done.8, bf16[64,32,256]{2,1,0:T(8,128)(2,1)S(1)} %gather_fusion.1, pred[64]{0:T(512)(128)(4,1)S(1)} %get-tuple-element.255), kind=kOutput, calls=%fused_computation.11.clone.1 | convolution fusion | flops 34736160 | bytes 2359424 | tf_op jit(solution)/shard_map/while/body/eval_jaxpr/div | solution.py:38
  75.9 0.1 constant_dynamic-slice_fusion.2
  76.0 0.8 copy.34
  76.8 2.5 %fusion.62 = f32[64,32,32]{2,1,0:T(8,128)S(1)} fusion(f32[64,32,32]{2,1,0:T(8,128)} %fusion.60, f32[64,32,32]{2,1,0:T(8,128)} %fusion.61, bf16[64,32,32]{2,1,0:T(8,128)(2,1)S(1)} %copy.34), kind=kOutput, calls=%fused_computation.17.clone.1 | output fusion | flops 460831 | bytes 917504 | tf_op jit(solution)/shard_map/while/body/eval_jaxpr/sub | solution.py:43
  79.3 5.0 %fusion.64 = f32[64,32,256]{2,1,0:T(8,128)} fusion(f32[64,32,32]{2,1,0:T(8,128)S(1)} %fusion.62, f32[64,32,32]{2,1,0:T(8,128)} %fusion.61, bf16[64,32,256]{2,1,0:T(8,128)(2,1)} %gather_fusion, pred[64]{0:T(512)(128)(4,1)S(1)} %copy-done.8, f32[64,32,32]{2,1,0:T(8,128)} %fusion.60, bf16[64,32,32]{2,1,0:T(8,128)(2,1)S(1)} %copy.34), kind=kOutput, calls=%fused_computation.29.clone.1 | convolution fusion | flops 34736160 | bytes 4063296 | tf_op jit(solution)/shard_map/while/body/eval_jaxpr/eij,eid->ejd/dot_general | solution.py:49
  84.4 7.0 %scatter_fusion.1 = f32[32,32,256]{2,1,0:T(8,128)S(1)} fusion(f32[32,32,256]{2,1,0:T(8,128)S(1)} %get-tuple-element.270, s32[64]{0:T(128)S(1)} %get-tuple-element.254, f32[64,32,256]{2,1,0:T(8,128)} %fusion.64), kind=kCustom, calls=%fused_computation.5.clone.1 | custom fusion | flops 524288 | bytes 6291712 | tf_op jit(solution)/shard_map/while/body/eval_jaxpr/scatter-add | solution.py:92
  91.4 5.3 %fusion.63 = f32[64,32,256]{2,1,0:T(8,128)} fusion(f32[64,32,32]{2,1,0:T(8,128)S(1)} %fusion.62, f32[64,32,32]{2,1,0:T(8,128)} %fusion.61, bf16[64,32,256]{2,1,0:T(8,128)(2,1)} %copy-done.1, pred[64]{0:T(512)(128)(4,1)S(1)} %get-tuple-element.255, f32[64,32,32]{2,1,0:T(8,128)} %fusion.60, bf16[64,32,32]{2,1,0:T(8,128)(2,1)S(1)} %copy.34), kind=kOutput, calls=%fused_computation.30.clone.1 | convolution fusion | flops 34736160 | bytes 4063296 | tf_op jit(solution)/shard_map/while/body/eval_jaxpr/eij,ejd->eid/dot_general | solution.py:46
  96.7 7.0 %scatter_fusion = f32[16,32,256]{2,1,0:T(8,128)S(1)} fusion(f32[16,32,256]{2,1,0:T(8,128)S(1)} %get-tuple-element.269, s32[64]{0:T(128)S(1)} %get-tuple-element.252, f32[64,32,256]{2,1,0:T(8,128)} %fusion.63), kind=kCustom, calls=%fused_computation.4.clone.1 | custom fusion | flops 524288 | bytes 6291712 | tf_op jit(solution)/shard_map/while/body/eval_jaxpr/scatter-add | solution.py:91
  103.8 0.0 copy-start.6
  103.8 0.0 copy-start.13
  103.8 0.9 convert_element_type.40
  104.7 3.5 %all-to-all-start.1 = ((bf16[32,32,256]{2,1,0:T(8,128)(2,1)}), bf16[32,32,256]{2,1,0:T(8,128)(2,1)S(1)}, u32[]{:S(2)}, u32[]{:S(2)}) async-start(bf16[32,32,256]{2,1,0:T(8,128)(2,1)} %convert_element_type.40), calls=%async_computation.2 | async-start | bytes 1048576 | tf_op jit(solution)/shard_map/all_to_all | solution.py:100
  108.2 0.0 reduce-scatter.2.cloned.1.call-start
  108.2 0.7 convert_element_type.38
  109.0 0.0 reduce-scatter.2.cloned.1.call-update
  109.0 0.3 multiply_reduce_fusion.4
  109.3 8.6 %all-to-all-done.1 = bf16[32,32,256]{2,1,0:T(8,128)(2,1)S(1)} async-done(((bf16[32,32,256]{2,1,0:T(8,128)(2,1)}), bf16[32,32,256]{2,1,0:T(8,128)(2,1)S(1)}, u32[]{:S(2)}, u32[]{:S(2)}) %all-to-all-start.1) | async-done | bytes 524320 | tf_op jit(solution)/shard_map/all_to_all | solution.py:100
  117.8 0.4 fusion.31
  118.2 12.9 %reduce-scatter.2.cloned.1.call-done = bf16[4,32,256]{2,1,0:T(8,128)(2,1)} async-done(((bf16[16,32,256]{2,1,0:T(8,128)(2,1)}), bf16[4,32,256]{2,1,0:T(8,128)(2,1)}) %reduce-scatter.2.cloned.1.call-update) | async-done | bytes 65552 | tf_op jit(solution)/shard_map/reduce_scatter | solution.py:103
  131.1 0.9 copy_add_fusion
  132.0 0.2 fusion.33
  132.1 0.1 fusion.35
  132.3 0.8 convolution_convert_fusion
  (48 shorter events, 0.2 us)
Async XLA Ops:
  6.5 20.5 %copy-start = (bf16[256,256]{1,0:T(8,128)(2,1)S(1)}, bf16[256,256]{1,0:T(8,128)(2,1)}, u32[]{:S(2)}) copy-start(bf16[256,256]{1,0:T(8,128)(2,1)} %param.9) | copy-start | bytes 393220
  6.5 19.9 %copy-start.5 = (bf16[4,32,256]{2,1,0:T(8,128)(2,1)S(1)}, bf16[4,32,256]{2,1,0:T(8,128)(2,1)}, u32[]{:S(2)}) copy-start(bf16[4,32,256]{2,1,0:T(8,128)(2,1)} %param.8) | copy-start | bytes 196612
  6.5 12.7 %copy-start.7 = (bf16[128,1024]{1,0:T(8,128)(2,1)S(1)}, bf16[128,1024]{1,0:T(8,128)(2,1)}, u32[]{:S(2)}) copy-start(bf16[128,1024]{1,0:T(8,128)(2,1)} %param.10) | copy-start | bytes 786436
  6.5 13.6 %collective-permute-start = (bf16[4,32,256]{2,1,0:T(8,128)(2,1)}, bf16[4,32,256]{2,1,0:T(8,128)(2,1)S(1)}, u32[]{:S(2)}, u32[]{:S(2)}) collective-permute-start(bf16[4,32,256]{2,1,0:T(8,128)(2,1)} %param.8), channel_id=1, source_target_pairs={{0,1},{1,2},{2,3},{3,0},{4,5},{5,6},{6,7},{7,4},{8,9},{9,10},{10,1... | collective-permute-start | bytes 196616 | tf_op jit(solution)/shard_map/ppermute | solution.py:64
  9.6 10.6 %collective-permute-start.2 = (bf16[4,32,256]{2,1,0:T(8,128)(2,1)}, bf16[4,32,256]{2,1,0:T(8,128)(2,1)S(1)}, u32[]{:S(2)}, u32[]{:S(2)}) collective-permute-start(bf16[4,32,256]{2,1,0:T(8,128)(2,1)} %param.8), channel_id=1, source_target_pairs={{1,0},{2,1},{3,2},{0,3},{5,4},{6,5},{7,6},{4,7},{9,8},{10,9},{11,1... | collective-permute-start | bytes 196616 | tf_op jit(solution)/shard_map/ppermute | solution.py:66
  15.3 13.6 %all-to-all-start = ((bf16[32,32,256]{2,1,0:T(8,128)(2,1)}), bf16[32,32,256]{2,1,0:T(8,128)(2,1)S(1)}, u32[]{:S(2)}, u32[]{:S(2)}) async-start(bf16[32,32,256]{2,1,0:T(8,128)(2,1)} %broadcast_select_fusion.6), calls=%async_computation | async-start | bytes 1048576 | tf_op jit(solution)/shard_map/all_to_all | solution.py:71
  20.1 6.3 %collective-permute-start.1 = (bf16[4,32,256]{2,1,0:T(8,128)(2,1)S(1)}, bf16[4,32,256]{2,1,0:T(8,128)(2,1)S(1)}, u32[]{:S(2)}, u32[]{:S(2)}) collective-permute-start(bf16[4,32,256]{2,1,0:T(8,128)(2,1)S(1)} %collective-permute-done), channel_id=1, source_target_pairs={{0,1},{1,2},{2,3},{3,0},{4,5},{5,6},{6,7},{7,4},{8,9},{9,10},{10,1... | collective-permute-start | bytes 196616 | tf_op jit(solution)/shard_map/ppermute | solution.py:64
  28.9 0.8 copy-start.9
  28.9 0.8 copy-start.11
  29.8 3.0 %copy-start.2 = (bf16[32,32,256]{2,1,0:T(8,128)(2,1)}, bf16[32,32,256]{2,1,0:T(8,128)(2,1)S(1)}, u32[]{:S(2)}) copy-start(bf16[32,32,256]{2,1,0:T(8,128)(2,1)S(1)} %get-tuple-element.286) | copy-start | bytes 1572868 | tf_op jit(solution)/shard_map/while
  32.8 3.3 %copy-start.1 = (bf16[64,32,256]{2,1,0:T(8,128)(2,1)}, bf16[64,32,256]{2,1,0:T(8,128)(2,1)S(1)}, u32[]{:S(2)}) copy-start(bf16[64,32,256]{2,1,0:T(8,128)(2,1)S(1)} %gather_fusion.1) | copy-start | bytes 3145732 | tf_op jit(solution)/shard_map/while
  32.8 3.3 %copy-start.8 = (pred[64]{0:T(512)(128)(4,1)S(1)}, pred[64]{0:T(512)(128)(4,1)}, u32[]{:S(2)}) copy-start(pred[64]{0:T(512)(128)(4,1)} %get-tuple-element.253) | copy-start | bytes 196 | tf_op jit(solution)/shard_map/while
  36.0 2.9 %copy-start.4 = (bf16[128,32,32]{0,2,1:T(8,128)(2,1)S(1)}, bf16[128,32,32]{0,2,1:T(8,128)(2,1)}, u32[]{:S(2)}) copy-start(bf16[128,32,32]{0,2,1:T(8,128)(2,1)} %get-tuple-element.287) | copy-start | bytes 786436 | tf_op jit(solution)/shard_map/while
  59.7 7.0 %copy-start.3 = (bf16[32,32,256]{2,1,0:T(8,128)(2,1)S(1)}, bf16[32,32,256]{2,1,0:T(8,128)(2,1)}, u32[]{:S(2)}) copy-start(bf16[32,32,256]{2,1,0:T(8,128)(2,1)} %copy-done.2) | copy-start | bytes 1572868 | tf_op jit(solution)/shard_map/while
  59.7 7.0 %copy-start.10 = (s32[128]{0:T(128)S(1)}, s32[128]{0:T(128)}, u32[]{:S(2)}) copy-start(s32[128]{0:T(128)} %get-tuple-element.316) | copy-start | bytes 1540 | tf_op jit(solution)/shard_map/while
  59.7 7.1 %copy-start.12 = (s32[128]{0:T(128)S(1)}, s32[128]{0:T(128)}, u32[]{:S(2)}) copy-start(s32[128]{0:T(128)} %get-tuple-element.330) | copy-start | bytes 1540 | tf_op jit(solution)/shard_map/while
  66.8 3.0 %copy-start.2 = (bf16[32,32,256]{2,1,0:T(8,128)(2,1)}, bf16[32,32,256]{2,1,0:T(8,128)(2,1)S(1)}, u32[]{:S(2)}) copy-start(bf16[32,32,256]{2,1,0:T(8,128)(2,1)S(1)} %get-tuple-element.286) | copy-start | bytes 1572868 | tf_op jit(solution)/shard_map/while
  69.8 3.3 %copy-start.1 = (bf16[64,32,256]{2,1,0:T(8,128)(2,1)}, bf16[64,32,256]{2,1,0:T(8,128)(2,1)S(1)}, u32[]{:S(2)}) copy-start(bf16[64,32,256]{2,1,0:T(8,128)(2,1)S(1)} %gather_fusion.1) | copy-start | bytes 3145732 | tf_op jit(solution)/shard_map/while
  69.8 3.3 %copy-start.8 = (pred[64]{0:T(512)(128)(4,1)S(1)}, pred[64]{0:T(512)(128)(4,1)}, u32[]{:S(2)}) copy-start(pred[64]{0:T(512)(128)(4,1)} %get-tuple-element.253) | copy-start | bytes 196 | tf_op jit(solution)/shard_map/while
  73.0 2.9 %copy-start.4 = (bf16[128,32,32]{0,2,1:T(8,128)(2,1)S(1)}, bf16[128,32,32]{0,2,1:T(8,128)(2,1)}, u32[]{:S(2)}) copy-start(bf16[128,32,32]{0,2,1:T(8,128)(2,1)} %get-tuple-element.287) | copy-start | bytes 786436 | tf_op jit(solution)/shard_map/while
  96.7 7.0 %copy-start.3 = (bf16[32,32,256]{2,1,0:T(8,128)(2,1)S(1)}, bf16[32,32,256]{2,1,0:T(8,128)(2,1)}, u32[]{:S(2)}) copy-start(bf16[32,32,256]{2,1,0:T(8,128)(2,1)} %copy-done.2) | copy-start | bytes 1572868 | tf_op jit(solution)/shard_map/while
  96.7 7.1 %copy-start.10 = (s32[128]{0:T(128)S(1)}, s32[128]{0:T(128)}, u32[]{:S(2)}) copy-start(s32[128]{0:T(128)} %get-tuple-element.316) | copy-start | bytes 1540 | tf_op jit(solution)/shard_map/while
  96.7 7.1 %copy-start.12 = (s32[128]{0:T(128)S(1)}, s32[128]{0:T(128)}, u32[]{:S(2)}) copy-start(s32[128]{0:T(128)} %get-tuple-element.330) | copy-start | bytes 1540 | tf_op jit(solution)/shard_map/while
  103.8 5.2 %copy-start.6 = (bf16[4,32,256]{2,1,0:T(8,128)(2,1)S(1)}, bf16[4,32,256]{2,1,0:T(8,128)(2,1)}, u32[]{:S(2)}) copy-start(bf16[4,32,256]{2,1,0:T(8,128)(2,1)} %param.8) | copy-start | bytes 196612
  103.8 14.0 %copy-start.13 = (s32[32]{0:T(128)S(1)}, s32[32]{0:T(128)}, u32[]{:S(2)}) copy-start(s32[32]{0:T(128)} %param.13) | copy-start | bytes 388
  104.7 13.1 %all-to-all-start.1 = ((bf16[32,32,256]{2,1,0:T(8,128)(2,1)}), bf16[32,32,256]{2,1,0:T(8,128)(2,1)S(1)}, u32[]{:S(2)}, u32[]{:S(2)}) async-start(bf16[32,32,256]{2,1,0:T(8,128)(2,1)} %convert_element_type.40), calls=%async_computation.2 | async-start | bytes 1048576 | tf_op jit(solution)/shard_map/all_to_all | solution.py:100
  108.2 22.9 %reduce-scatter.2.cloned.1.call-start = ((), (), s32[]{:S(2)}) async-start(), calls=%async_computation.3 | async-start | bytes 327680 | tf_op jit(solution)/shard_map/reduce_scatter | solution.py:103
Sparse Core Ops, SparseCore 0:
  111.2 19.8 reduce-scatter.1
